TPU v7x, 512 devices: a whole 4x8x8 slice. The times are simulated.
512 devices in a mesh: lat: 16 (over y_hi, x, core), lon: 32 (over z, y_lo).
Axes of the slice: x: 4, y: 8 (y_hi: 2, y_lo: 4; y = y_hi * 4 + y_lo), z: 8, core: 2. Of those that a mesh axis runs over, the one named last changes fastest.
Arguments:
- queries: bfloat16 [131072, 1024], P(('lat', 'lon')), may hold values from -6 to 6
- gain: bfloat16 [1024], replicated, may hold values from 0.099609375 to 1.8984375
- w_query: bfloat16 [1024, 1024], P('lon'), may hold values from -0.1875 to 0.1875
- w_out: bfloat16 [1024, 1024], P(None, 'lon'), may hold values from -0.75 to 0.75
- kv_cache: bfloat16 [2, 32, 256, 1024], P(None, 'lat'), may hold values from -60 to 60
- nbr_lists: int32 [512, 4], P(('lat', 'lon')), may hold values from 0 to 31, as said below
- counts: int32 [512], P(('lat', 'lon')), may hold values from 1 to 4, as said below
Outputs:
- decoded: bfloat16 [131072, 1024], P(('lat', 'lon'))
Inputs may be any that keep to these rules, and one draw needn't show every extreme that they name: `nbr_lists`: query block b lies in band b // 32; band k holds latent blocks k * 2 to (k+1) * 2 - 1. Entries of b's list lie in its band or the bands beside it; its first counts[b] entries differ, the others repeat entry 0. `counts`: query blocks of the first and last band have 4 valid slots.
All inputs are finite; a program needn't handle non-finite values.
Results may differ from a plain program's by a relative error of at most 0.007.
The roundings to bfloat16 on the way count: a program that leaves them out, or rounds other values in their place, can miss the bound.
Values may be sent and summed in bfloat16 or wider, within the bound.
No kernel may reach another device: no remote copies, remote signals or barrier semaphores. Data moves between devices by JAX's collectives and lax.ppermute only.
A program may use at most 64 MiB of HBM per device.

v0:
```python
import jax
import jax.numpy as jnp
from jax import lax
from jax.sharding import PartitionSpec as P

H = 16
HD = 64
BLOCK_TOKENS = 256


def padded(array, sides, width):
    for axis, dim in sides:
        devices, length = (lax.axis_size(axis), array.shape[dim])
        up = [(i, (i + 1) % devices) for i in range(devices - 1)]
        down = [(j, i) for i, j in up]
        last = lax.slice_in_dim(array, length - width, length, axis=dim)
        initial = lax.slice_in_dim(array, 0, width, axis=dim)
        before = lax.ppermute(last, axis, up)
        after = lax.ppermute(initial, axis, down)
        array = jnp.concatenate([before, array, after], axis=dim)
    return array


def on_device(queries, gain, w_query, w_out, kv_cache, nbr_lists, counts):
    rows = queries.astype(jnp.float32)
    rowwise_scale = lax.rsqrt(jnp.mean(rows * rows, axis=1, keepdims=True) + 1e-05)
    normed = (rows * rowwise_scale * gain.astype(jnp.float32)[None, :]).astype(jnp.bfloat16)
    row_count = queries.shape[0]
    query_count = row_count // BLOCK_TOKENS
    projected = jnp.dot(
        normed,
        lax.all_gather(w_query, "lon", axis=0, tiled=True),
        preferred_element_type=jnp.float32,
    )
    query = (projected * HD ** (-0.5)).astype(jnp.bfloat16)
    q_heads = query.reshape(query_count, BLOCK_TOKENS, H, HD)
    lat_index = lax.axis_index("lat")
    blocks_here = kv_cache.shape[1]
    window = padded(kv_cache, (("lat", 1),), blocks_here)
    key_window = window[0].reshape(3 * blocks_here, BLOCK_TOKENS, H, HD)
    value_window = window[1].reshape(3 * blocks_here, BLOCK_TOKENS, H, HD)
    local_lists = nbr_lists - (lat_index - 1) * blocks_here

    def update(state, scores, is_live, value_rows, value_form):
        best, total_sum, running = state
        peak = jnp.max(scores, axis=3)
        new_best = jnp.where(is_live[:, None, None], jnp.maximum(best, peak), best)
        rescale = jnp.exp(best - new_best)
        expo = jnp.where(is_live[:, None, None, None], jnp.exp(scores - new_best[..., None]), 0.0)
        total_sum = total_sum * rescale + jnp.sum(expo, axis=3)
        mixed = jnp.einsum(
            value_form, expo.astype(jnp.bfloat16), value_rows, preferred_element_type=jnp.float32
        )
        running = running * rescale[..., None] + mixed
        return (new_best, total_sum, running)

    start_state = (
        jnp.full((query_count, BLOCK_TOKENS, H), -1e30, jnp.float32),
        jnp.zeros((query_count, BLOCK_TOKENS, H), jnp.float32),
        jnp.zeros((query_count, BLOCK_TOKENS, H, HD), jnp.float32),
    )

    def listed_step(slot_index, state):
        picked = lax.dynamic_slice_in_dim(local_lists, slot_index, 1, 1)[:, 0]
        key_rows = jnp.take(key_window, picked, axis=0)
        value_rows = jnp.take(value_window, picked, axis=0)
        scores = jnp.einsum(
            "bqhd,bkhd->bqhk", q_heads, key_rows, preferred_element_type=jnp.float32
        )
        return update(state, scores, slot_index < counts, value_rows, "bqhk,bkhd->bqhd")

    final_state = lax.fori_loop(0, jnp.max(counts), listed_step, start_state)
    attended = (
        (final_state[2] / final_state[1][..., None]).reshape(row_count, H * HD).astype(jnp.bfloat16)
    )
    decoded = jnp.dot(
        attended,
        lax.all_gather(w_out, "lon", axis=1, tiled=True),
        preferred_element_type=jnp.float32,
    )
    return decoded.astype(jnp.bfloat16)


def solution(mesh):
    placed = (
        P(("lat", "lon"), None),
        P(),
        P("lon", None),
        P(None, "lon"),
        P(None, "lat", None, None),
        P(("lat", "lon"), None),
        P(("lat", "lon")),
    )
    return jax.shard_map(
        on_device, mesh=mesh, in_specs=placed, out_specs=P(("lat", "lon"), None), check_vma=False
    )
```

profile of v0, /device:TPU:6, one launch (start us, length us, event | category | flops | bytes accessed | tf_op | source)
XLA Modules:
  0.0 351.9 jit_solution(9030099862044191392)
XLA Ops:
  6.5 0.0 copy-start
  6.5 0.0 all-gather.3.cloned.1.call-start
  6.5 0.7 all-gather.3.cloned.1.call-update
  7.3 0.0 all-gather.5.cloned.1.call-start
  7.3 1.9 collective-permute-start
  9.2 3.6 %collective-permute-start.1 = (bf16[2,2,256,1024]{3,2,1,0:T(8,128)(2,1)}, bf16[2,2,256,1024]{3,2,1,0:T(8,128)(2,1)}, u32[]{:S(2)}, u32[]{:S(2)}) collective-permute-start(bf16[2,2,256,1024]{3,2,1,0:T(8,128)(2,1)} %param.15), channel_id=1, source_target_pairs={{32,0},{64,32},{96,64},{128,96},{160,128},{192,160},{224,192},{256... | collective-permute-start | bytes 6291464 | tf_op jit(solution)/shard_map/ppermute | solution.py:19
  12.9 0.0 all-gather.5.cloned.1.call-update
  12.9 0.7 convert_element_type.25
  13.6 1.2 fusion.35
  14.8 0.7 broadcast_subtract_fusion
  15.5 19.5 %collective-permute-done = bf16[2,2,256,1024]{3,2,1,0:T(8,128)(2,1)} collective-permute-done((bf16[2,2,256,1024]{3,2,1,0:T(8,128)(2,1)}, bf16[2,2,256,1024]{3,2,1,0:T(8,128)(2,1)}, u32[]{:S(2)}, u32[]{:S(2)}) %collective-permute-start) | collective-permute-done | bytes 2097184 | tf_op jit(solution)/shard_map/ppermute | solution.py:18
  35.0 1.8 constant_dynamic-update-slice_fusion.2
  36.7 0.0 copy-done
  36.7 0.2 constant_dynamic-update-slice_fusion.1
  36.9 0.0 collective-permute-done.1
  36.9 1.8 constant_dynamic-update-slice_fusion
  38.7 2.7 fusion.41
  41.5 4.7 %copy.13 = bf16[1,6,256,1024]{2,3,1,0:T(8,128)(2,1)} copy(bf16[1,6,256,1024]{3,2,1,0:T(8,128)(2,1)} %get-tuple-element.108) | data formatting | bytes 6291456 | tf_op jit(solution)/shard_map/slice | solution.py:40
  46.1 2.8 copy.15
  48.9 131.5 %all-gather.3.cloned.1.call-done = bf16[1024,1024]{1,0:T(8,128)(2,1)} async-done(((bf16[32,1024]{1,0:T(8,128)(2,1)}), bf16[1024,1024]{1,0:T(8,128)(2,1)}) %all-gather.3.cloned.1.call-update) | async-done | bytes 2097168 | tf_op jit(solution)/shard_map/all_gather | solution.py:32
  180.5 2.5 fusion.34
  183.0 0.2 copy.14
  183.2 0.1 broadcast_in_dim.49
  183.4 9.0 %while.15 = (s32[]{:T(128)}, f32[1,256,16]{1,2,0:T(8,128)S(1)}, f32[1,256,16]{1,2,0:T(8,128)S(1)}, f32[1,256,16,64]{1,3,2,0:T(8,128)S(1)}, s32[]{:T(128)}, /*ind...) while((s32[]{:T(128)}, f32[1,256,16]{1,2,0:T(8,128)S(1)}, ...), condition=%wide.region_4.0_spmd, body=%wide.region_1.5_spmd.sunk | while | flops 276840448 | bytes 16517893 | solution.py:72
  184.0 0.6 constant_dynamic-slice_fusion.2
  186.5 1.8 bitcast_reduce_fusion.2
  189.0 2.0 fusion.54
  191.0 0.7 fusion.53
  192.4 0.1 divide_convert_fusion
  192.5 149.4 %all-gather.5.cloned.1.call-done = bf16[1024,1024]{0,1:T(8,128)(2,1)} async-done(((bf16[1024,32]{0,1:T(8,128)(2,1)}), bf16[1024,1024]{0,1:T(8,128)(2,1)}) %all-gather.5.cloned.1.call-update) | async-done | bytes 2097168 | tf_op jit(solution)/shard_map/all_gather | solution.py:78
  341.9 3.1 convolution_convert_fusion
  (6 shorter events, 0.0 us)
Async XLA Ops:
  6.5 30.2 %copy-start = (bf16[2,2,256,1024]{3,2,1,0:T(8,128)(2,1)S(1)}, bf16[2,2,256,1024]{3,2,1,0:T(8,128)(2,1)}, u32[]{:S(2)}) copy-start(bf16[2,2,256,1024]{3,2,1,0:T(8,128)(2,1)} %param.15) | copy-start | bytes 6291460
  6.5 173.9 %all-gather.3.cloned.1.call-start = ((), (), s32[]{:S(2)}) async-start(), calls=%async_computation | async-start | bytes 2162688 | tf_op jit(solution)/shard_map/all_gather | solution.py:32
  7.3 334.7 %all-gather.5.cloned.1.call-start = ((), (), s32[]{:S(2)}) async-start(), calls=%async_computation.1 | async-start | bytes 2162688 | tf_op jit(solution)/shard_map/all_gather | solution.py:78
  7.3 27.7 %collective-permute-start = (bf16[2,2,256,1024]{3,2,1,0:T(8,128)(2,1)}, bf16[2,2,256,1024]{3,2,1,0:T(8,128)(2,1)}, u32[]{:S(2)}, u32[]{:S(2)}) collective-permute-start(bf16[2,2,256,1024]{3,2,1,0:T(8,128)(2,1)} %param.15), channel_id=1, source_target_pairs={{0,32},{32,64},{64,96},{96,128},{128,160},{160,192},{192,224},{224... | collective-permute-start | bytes 6291464 | tf_op jit(solution)/shard_map/ppermute | solution.py:18
  9.2 27.7 %collective-permute-start.1 = (bf16[2,2,256,1024]{3,2,1,0:T(8,128)(2,1)}, bf16[2,2,256,1024]{3,2,1,0:T(8,128)(2,1)}, u32[]{:S(2)}, u32[]{:S(2)}) collective-permute-start(bf16[2,2,256,1024]{3,2,1,0:T(8,128)(2,1)} %param.15), channel_id=1, source_target_pairs={{32,0},{64,32},{96,64},{128,96},{160,128},{192,160},{224,192},{256... | collective-permute-start | bytes 6291464 | tf_op jit(solution)/shard_map/ppermute | solution.py:19
Sparse Core Ops, SparseCore 0:
  9.4 171.0 all-gather.2
  182.6 159.3 all-gather.4
where the time goes:
time: 353 us; the launch traced here: 352 us
  waiting for transfers between devices  301 us (85%)
  local copies, waits for them, and re-layouts  14.9 us (4%)
  between operations  13.5 us (4%)
  matrix products  9.45 us (3%)
  starting transfers between devices  5.6 us (2%)
  loops' own time  3.89 us (1%)
    all_gather x1, waiting for transfers between devices, on_device(): lax.all_gather(w_out, 'lon', axis=1, tiled=True)  149 us
    all_gather x1, waiting for transfers between devices, on_device(): lax.all_gather(w_query, 'lon', axis=0, tiled=True)  132 us
    ppermute x1, waiting for transfers between devices, padded(): before = lax.ppermute(last, axis, up)  19.5 us
  transfers between devices with their start and end apart: 4, of which 3 were waited for; matrix products, arithmetic and copies ran while one was open for 7% of the time, Pallas kernels for 0%

commit v1 on v0

--- a/solution.py
+++ b/solution.py
@@ -21,6 +21,20 @@
     return array
 
 
+def gathered_rows(local):
+    lon_count = lax.axis_size("lon")
+    core = lax.axis_index("lat") % 2
+    half = local.shape[1] // 2
+    mine = lax.dynamic_slice_in_dim(local, core * half, half, axis=1)
+    fetched = lax.all_to_all(jnp.tile(mine, (lon_count, 1)), "lon", 0, 0, tiled=True)
+    lat_count = lax.axis_size("lat")
+    swap = [(i, i ^ 1) for i in range(lat_count)]
+    other = lax.ppermute(fetched, "lat", swap)
+    low = jnp.where(core == 0, fetched, other)
+    high = jnp.where(core == 0, other, fetched)
+    return jnp.concatenate([low, high], axis=1)
+
+
 def on_device(queries, gain, w_query, w_out, kv_cache, nbr_lists, counts):
     rows = queries.astype(jnp.float32)
     rowwise_scale = lax.rsqrt(jnp.mean(rows * rows, axis=1, keepdims=True) + 1e-05)
@@ -29,7 +43,7 @@
     query_count = row_count // BLOCK_TOKENS
     projected = jnp.dot(
         normed,
-        lax.all_gather(w_query, "lon", axis=0, tiled=True),
+        gathered_rows(w_query),
         preferred_element_type=jnp.float32,
     )
     query = (projected * HD ** (-0.5)).astype(jnp.bfloat16)
@@ -73,9 +87,10 @@
     attended = (
         (final_state[2] / final_state[1][..., None]).reshape(row_count, H * HD).astype(jnp.bfloat16)
     )
-    decoded = jnp.dot(
+    decoded = lax.dot_general(
         attended,
-        lax.all_gather(w_out, "lon", axis=1, tiled=True),
+        gathered_rows(w_out.T),
+        (((1,), (1,)), ((), ())),
         preferred_element_type=jnp.float32,
     )
     return decoded.astype(jnp.bfloat16)

time: 353 us -> 175 us (0.50)
  the two profiles are of different devices: /device:TPU:6 before, /device:TPU:176 now
where the time goes in v1:
time: 175 us; the launch traced here: 173 us
  waiting for transfers between devices  79.5 us (45%)
  starting transfers between devices  33.4 us (19%)
  local copies, waits for them, and re-layouts  20.6 us (12%)
  matrix products  18.7 us (11%)
  loops' own time  14.2 us (8%)
  other arithmetic  6.76 us (4%)
    all_to_all x2, waiting for transfers between devices, gathered_rows(): lax.all_to_all(jnp.tile(mine, (lon_count, 1)), 'lon', 0, 0, tiled=True)  61.6 us
    all_to_all x2, starting transfers between devices, gathered_rows(): lax.all_to_all(jnp.tile(mine, (lon_count, 1)), 'lon', 0, 0, tiled=True)  18 us
    ppermute x1, waiting for transfers between devices, padded(): before = lax.ppermute(last, axis, up)  18 us
    another operation x1, loops' own time, on_device(): final_state = lax.fori_loop(0, jnp.max(counts), listed_step, start_state)  14.2 us
    ppermute x1, starting transfers between devices, padded(): after = lax.ppermute(initial, axis, down)  9.66 us
    dot_general x4, matrix products, update(): jnp.einsum(value_form, expo.astype(jnp.bfloat16), value_rows, preferred_e...  7.88 us
    dot_general x4, matrix products, listed_step(): jnp.einsum('bqhd,bkhd->bqhk', q_heads, key_rows, preferred_element_type=j...  7.23 us
    slice x2, local copies, waits for them, and re-layouts, on_device(): value_window = window[1].reshape(3 * blocks_here, BLOCK_TOKENS, H, HD)  5.55 us
  transfers between devices with their start and end apart: 6, of which 3 were waited for; matrix products, arithmetic and copies ran while one was open for 9% of the time, Pallas kernels for 0%

profile of v1, /device:TPU:176, one launch (start us, length us, event | category | flops | bytes accessed | tf_op | source)
XLA Modules:
  0.0 173.4 jit_solution(17049636063988587741)
XLA Ops:
  0.0 0.0 copy-start.5
  0.0 0.0 copy-start.4
  0.1 0.8 copy-done
  0.8 1.1 tile.5
  1.9 11.2 %all-to-all-start.1 = ((bf16[32,32,512]{2,1,0:T(8,128)(2,1)}), bf16[32,32,512]{2,1,0:T(8,128)(2,1)}, u32[]{:S(2)}, u32[]{:S(2)}) async-start(bf16[32,32,512]{2,1,0:T(8,128)(2,1)} %tile.5), calls=%async_computation.1 | async-start | bytes 2097152 | tf_op jit(solution)/shard_map/all_to_all | solution.py:29
  13.1 0.8 constant_dynamic-slice_fusion.1
  13.9 26.3 %all-to-all-done.1 = bf16[32,32,512]{2,1,0:T(8,128)(2,1)} async-done(((bf16[32,32,512]{2,1,0:T(8,128)(2,1)}), bf16[32,32,512]{2,1,0:T(8,128)(2,1)}, u32[]{:S(2)}, u32[]{:S(2)}) %all-to-all-start.1) | async-done | bytes 1048608 | tf_op jit(solution)/shard_map/all_to_all | solution.py:29
  40.2 1.1 tile.4
  41.3 6.8 %all-to-all-start = ((bf16[32,32,512]{2,1,0:T(8,128)(2,1)}), bf16[32,32,512]{2,1,0:T(8,128)(2,1)}, u32[]{:S(2)}, u32[]{:S(2)}) async-start(bf16[32,32,512]{2,1,0:T(8,128)(2,1)} %tile.4), calls=%async_computation | async-start | bytes 2097152 | tf_op jit(solution)/shard_map/all_to_all | solution.py:29
  48.1 1.9 %collective-permute-start = (bf16[2,2,256,1024]{3,2,1,0:T(8,128)(2,1)S(1)}, bf16[2,2,256,1024]{3,2,1,0:T(8,128)(2,1)}, u32[]{:S(2)}, u32[]{:S(2)}) collective-permute-start(bf16[2,2,256,1024]{3,2,1,0:T(8,128)(2,1)S(1)} %copy-done.1), channel_id=1, source_target_pairs={{0,32},{32,64},{64,96},{96,128},{128,160},{160,192},{192,224},{224... | collective-permute-start | bytes 6291464 | tf_op jit(solution)/shard_map/ppermute | solution.py:18
  50.1 9.7 %collective-permute-start.1 = (bf16[2,2,256,1024]{3,2,1,0:T(8,128)(2,1)S(1)}, bf16[2,2,256,1024]{3,2,1,0:T(8,128)(2,1)}, u32[]{:S(2)}, u32[]{:S(2)}) collective-permute-start(bf16[2,2,256,1024]{3,2,1,0:T(8,128)(2,1)S(1)} %copy-done.1), channel_id=1, source_target_pairs={{32,0},{64,32},{96,64},{128,96},{160,128},{192,160},{224,192},{256... | collective-permute-start | bytes 6291464 | tf_op jit(solution)/shard_map/ppermute | solution.py:19
  59.8 0.2 fusion.51
  60.0 1.9 %collective-permute-start.3 = (bf16[1024,512]{1,0:T(8,128)(2,1)}, bf16[1024,512]{1,0:T(8,128)(2,1)}, u32[]{:S(2)}, u32[]{:S(2)}) collective-permute-start(bf16[1024,512]{1,0:T(8,128)(2,1)} %bitcast.28), channel_id=1, source_target_pairs={{0,32},{32,0},{64,96},{96,64},{128,160},{160,128},{192,224},{224,1... | collective-permute-start | bytes 3145736 | tf_op jit(solution)/shard_map/ppermute | solution.py:32
  61.9 35.2 %all-to-all-done = bf16[32,32,512]{2,1,0:T(8,128)(2,1)} async-done(((bf16[32,32,512]{2,1,0:T(8,128)(2,1)}), bf16[32,32,512]{2,1,0:T(8,128)(2,1)}, u32[]{:S(2)}, u32[]{:S(2)}) %all-to-all-start) | async-done | bytes 1048608 | tf_op jit(solution)/shard_map/all_to_all | solution.py:29
  97.1 1.9 %collective-permute-start.2 = (bf16[1024,512]{1,0:T(8,128)(2,1)}, bf16[1024,512]{1,0:T(8,128)(2,1)}, u32[]{:S(2)}, u32[]{:S(2)}) collective-permute-start(bf16[1024,512]{1,0:T(8,128)(2,1)} %bitcast.22), channel_id=1, source_target_pairs={{0,32},{32,0},{64,96},{96,64},{128,160},{160,128},{192,224},{224,1... | collective-permute-start | bytes 3145736 | tf_op jit(solution)/shard_map/ppermute | solution.py:32
  99.1 18.0 %collective-permute-done = bf16[2,2,256,1024]{3,2,1,0:T(8,128)(2,1)} collective-permute-done((bf16[2,2,256,1024]{3,2,1,0:T(8,128)(2,1)S(1)}, bf16[2,2,256,1024]{3,2,1,0:T(8,128)(2,1)}, u32[]{:S(2)}, u32[]{:S(2)}) %collective-permute-start) | collective-permute-done | bytes 2097184 | tf_op jit(solution)/shard_map/ppermute | solution.py:18
  117.1 1.8 %constant_dynamic-update-slice_fusion.2 = bf16[2,6,256,1024]{3,2,1,0:T(8,128)(2,1)S(1)} fusion(bf16[2,2,256,1024]{3,2,1,0:T(8,128)(2,1)} %collective-permute-done), kind=kLoop, calls=%fused_computation.61 | loop fusion | bytes 4194304
  118.8 0.2 constant_dynamic-update-slice_fusion.1
  119.0 0.0 collective-permute-done.1
  119.0 1.8 %constant_dynamic-update-slice_fusion = bf16[2,6,256,1024]{3,2,1,0:T(8,128)(2,1)S(1)} fusion(bf16[2,6,256,1024]{3,2,1,0:T(8,128)(2,1)S(1)} %constant_dynamic-update-slice_fusion.1, bf16[2,2,256,1024]{3,2,1,0:T(8,128)(2,1)} %collective-permute-done.1), kind=kLoop, calls=%fused_computation.59 | loop fusion | bytes 4194304 | tf_op jit(solution)/shard_map/concatenate | solution.py:20
  120.8 2.7 %fusion.59 = (bf16[1,6,256,1024]{3,2,1,0:T(8,128)(2,1)S(1)}, bf16[1,6,256,1024]{3,2,1,0:T(8,128)(2,1)}) fusion(bf16[2,6,256,1024]{3,2,1,0:T(8,128)(2,1)S(1)} %constant_dynamic-update-slice_fusion), kind=kLoop, calls=%fused_computation.67 | loop fusion | bytes 12582912 | tf_op jit(solution)/shard_map/slice | solution.py:55
  123.5 4.7 %copy.13 = bf16[1,6,256,1024]{2,3,1,0:T(8,128)(2,1)} copy(bf16[1,6,256,1024]{3,2,1,0:T(8,128)(2,1)} %get-tuple-element.108) | data formatting | bytes 6291456 | tf_op jit(solution)/shard_map/slice | solution.py:54
  128.2 2.8 %copy.15 = bf16[1,6,256,1024]{2,3,1,0:T(8,128)(2,1)} copy(bf16[1,6,256,1024]{3,2,1,0:T(8,128)(2,1)S(1)} %get-tuple-element.107) | data formatting | bytes 6291456 | tf_op jit(solution)/shard_map/slice | solution.py:55
  131.0 0.0 collective-permute-done.3
  131.0 0.0 collective-permute-done.2
  131.0 3.5 %broadcast_select_fusion.1 = (bf16[1024,512]{1,0:T(8,128)(2,1)S(1)}, bf16[1024,512]{1,0:T(8,128)(2,1)}, bf16[1024,512]{1,0:T(8,128)(2,1)S(1)}, bf16[1024,512]{1,0:T(8,128)(2,1)S(1)}) fusion(bf16[1024,512]{1,0:T(8,128)(2,1)} %collective-permute-done.3, pred[]{:T(512)S(6)} %eq.5, bf16[32,32,512]{2,1,0:T(8,128)(2,1)} %all-to-all-done.1, ...), kind=kLoop, calls=%fused_computation.53 | loop fusion | flops 2097152 | bytes 8388609 | tf_op jit(solution)/shard_map/jit(_where)/select_n | solution.py:33
  134.5 0.8 fusion.45
  135.3 0.2 copy.14
  135.5 0.1 broadcast_in_dim.49
  135.6 34.9 %while.15 = (s32[]{:T(128)}, f32[1,256,16]{1,2,0:T(8,128)S(1)}, f32[1,256,16]{1,2,0:T(8,128)S(1)}, f32[1,256,16,64]{1,3,2,0:T(8,128)S(1)}, s32[]{:T(128)}, /*ind...) while((s32[]{:T(128)}, f32[1,256,16]{1,2,0:T(8,128)S(1)}, ...), condition=%wide.region_4.6_spmd, body=%wide.region_1.0_spmd.sunk | while | flops 276840448 | bytes 16517901 | solution.py:86
  136.3 0.6 constant_dynamic-slice_fusion.3
  139.0 1.8 %bitcast_reduce_fusion.2 = (f32[256,16]{0,1:T(8,128)S(1)}, f32[16,256,256]{2,1,0:T(8,128)S(1)}) fusion(bf16[1,256,16,64]{1,3,2,0:T(8,128)(2,1)S(1)} %get-tuple-element.225, bf16[6,256,16,64]{1,3,2,0:T(8,128)(2,1)} %get-tuple-element.224, s32[]{:T(128)} %bitcast.103, pred[]{:T(512)} %bitcast.104), kind=kOutput, calls=%fused_computation.1.clone.1 | convolution fusion | flops 135524352 | bytes 5260288 | tf_op jit(solution)/shard_map/while/body/bqhd,bkhd->bqhk/dot_general | solution.py:81
  141.4 0.7 fusion.69
  142.2 2.0 %fusion.70 = f32[1,256,16,64]{1,3,2,0:T(8,128)S(1)} fusion(f32[16,256,256]{2,1,0:T(8,128)S(1)} %get-tuple-element.183, f32[256,16]{0,1:T(8,128)S(1)} %bitcast.112, pred[]{:T(512)} %bitcast.106, f32[1,256,16,64]{1,3,2,0:T(8,128)S(1)} %get-tuple-element.204, bf16[6,256,16,64]{1,3,2,0:T(8,128)(2,1)} %get-tuple-element.226, s32[]{:T(128)} %bitcast.103, ...), kind=kOutput, calls=%fused_computation.12.clone.1 | convolution fusion | flops 138149888 | bytes 6850048 | tf_op jit(solution)/shard_map/while/body/bqhk,bkhd->bqhd/dot_general | solution.py:65
  144.8 0.6 constant_dynamic-slice_fusion.3
  147.5 1.8 %bitcast_reduce_fusion.2 = (f32[256,16]{0,1:T(8,128)S(1)}, f32[16,256,256]{2,1,0:T(8,128)S(1)}) fusion(bf16[1,256,16,64]{1,3,2,0:T(8,128)(2,1)S(1)} %get-tuple-element.225, bf16[6,256,16,64]{1,3,2,0:T(8,128)(2,1)} %get-tuple-element.224, s32[]{:T(128)} %bitcast.103, pred[]{:T(512)} %bitcast.104), kind=kOutput, calls=%fused_computation.1.clone.1 | convolution fusion | flops 135524352 | bytes 5260288 | tf_op jit(solution)/shard_map/while/body/bqhd,bkhd->bqhk/dot_general | solution.py:81
  150.0 0.7 fusion.69
  150.8 2.0 %fusion.70 = f32[1,256,16,64]{1,3,2,0:T(8,128)S(1)} fusion(f32[16,256,256]{2,1,0:T(8,128)S(1)} %get-tuple-element.183, f32[256,16]{0,1:T(8,128)S(1)} %bitcast.112, pred[]{:T(512)} %bitcast.106, f32[1,256,16,64]{1,3,2,0:T(8,128)S(1)} %get-tuple-element.204, bf16[6,256,16,64]{1,3,2,0:T(8,128)(2,1)} %get-tuple-element.226, s32[]{:T(128)} %bitcast.103, ...), kind=kOutput, calls=%fused_computation.12.clone.1 | convolution fusion | flops 138149888 | bytes 6850048 | tf_op jit(solution)/shard_map/while/body/bqhk,bkhd->bqhd/dot_general | solution.py:65
  153.4 0.6 constant_dynamic-slice_fusion.3
  156.1 1.8 %bitcast_reduce_fusion.2 = (f32[256,16]{0,1:T(8,128)S(1)}, f32[16,256,256]{2,1,0:T(8,128)S(1)}) fusion(bf16[1,256,16,64]{1,3,2,0:T(8,128)(2,1)S(1)} %get-tuple-element.225, bf16[6,256,16,64]{1,3,2,0:T(8,128)(2,1)} %get-tuple-element.224, s32[]{:T(128)} %bitcast.103, pred[]{:T(512)} %bitcast.104), kind=kOutput, calls=%fused_computation.1.clone.1 | convolution fusion | flops 135524352 | bytes 5260288 | tf_op jit(solution)/shard_map/while/body/bqhd,bkhd->bqhk/dot_general | solution.py:81
  158.6 0.7 fusion.69
  159.3 2.0 %fusion.70 = f32[1,256,16,64]{1,3,2,0:T(8,128)S(1)} fusion(f32[16,256,256]{2,1,0:T(8,128)S(1)} %get-tuple-element.183, f32[256,16]{0,1:T(8,128)S(1)} %bitcast.112, pred[]{:T(512)} %bitcast.106, f32[1,256,16,64]{1,3,2,0:T(8,128)S(1)} %get-tuple-element.204, bf16[6,256,16,64]{1,3,2,0:T(8,128)(2,1)} %get-tuple-element.226, s32[]{:T(128)} %bitcast.103, ...), kind=kOutput, calls=%fused_computation.12.clone.1 | convolution fusion | flops 138149888 | bytes 6850048 | tf_op jit(solution)/shard_map/while/body/bqhk,bkhd->bqhd/dot_general | solution.py:65
  162.0 0.6 constant_dynamic-slice_fusion.3
  164.6 1.8 %bitcast_reduce_fusion.2 = (f32[256,16]{0,1:T(8,128)S(1)}, f32[16,256,256]{2,1,0:T(8,128)S(1)}) fusion(bf16[1,256,16,64]{1,3,2,0:T(8,128)(2,1)S(1)} %get-tuple-element.225, bf16[6,256,16,64]{1,3,2,0:T(8,128)(2,1)} %get-tuple-element.224, s32[]{:T(128)} %bitcast.103, pred[]{:T(512)} %bitcast.104), kind=kOutput, calls=%fused_computation.1.clone.1 | convolution fusion | flops 135524352 | bytes 5260288 | tf_op jit(solution)/shard_map/while/body/bqhd,bkhd->bqhk/dot_general | solution.py:81
  167.1 0.7 fusion.69
  167.9 2.0 %fusion.70 = f32[1,256,16,64]{1,3,2,0:T(8,128)S(1)} fusion(f32[16,256,256]{2,1,0:T(8,128)S(1)} %get-tuple-element.183, f32[256,16]{0,1:T(8,128)S(1)} %bitcast.112, pred[]{:T(512)} %bitcast.106, f32[1,256,16,64]{1,3,2,0:T(8,128)S(1)} %get-tuple-element.204, bf16[6,256,16,64]{1,3,2,0:T(8,128)(2,1)} %get-tuple-element.226, s32[]{:T(128)} %bitcast.103, ...), kind=kOutput, calls=%fused_computation.12.clone.1 | convolution fusion | flops 138149888 | bytes 6850048 | tf_op jit(solution)/shard_map/while/body/bqhk,bkhd->bqhd/dot_general | solution.py:65
  170.5 0.1 divide_convert_fusion
  170.6 2.8 %fusion.48 = bf16[256,1024]{1,0:T(8,128)(2,1)} fusion(bf16[256,1024]{0,1:T(8,128)(2,1)S(1)} %bitcast.114, bf16[1024,512]{1,0:T(8,128)(2,1)} %get-tuple-element.110, bf16[1024,512]{1,0:T(8,128)(2,1)S(1)} %get-tuple-element.109), kind=kOutput, calls=%fused_computation.47 | convolution fusion | flops 541327360 | bytes 3145728 | tf_op jit(solution)/shard_map/dot_general | solution.py:90
  (27 shorter events, 0.2 us)
Async XLA Ops:
  0.0 0.8 copy-start
  0.0 48.1 %copy-start.1 = (bf16[2,2,256,1024]{3,2,1,0:T(8,128)(2,1)S(1)}, bf16[2,2,256,1024]{3,2,1,0:T(8,128)(2,1)}, u32[]{:S(2)}) copy-start(bf16[2,2,256,1024]{3,2,1,0:T(8,128)(2,1)} %param.15) | copy-start | bytes 6291460
  0.0 59.7 %copy-start.2 = (bf16[256,1024]{1,0:T(8,128)(2,1)S(1)}, bf16[256,1024]{1,0:T(8,128)(2,1)}, u32[]{:S(2)}) copy-start(bf16[256,1024]{1,0:T(8,128)(2,1)} %param.11) | copy-start | bytes 1572868
  0.0 99.0 %copy-start.5 = (s32[1,4]{1,0:T(1,128)S(1)}, s32[1,4]{1,0:T(1,128)}, u32[]{:S(2)}) copy-start(s32[1,4]{1,0:T(1,128)} %param.16) | copy-start | bytes 52
  0.0 99.0 %copy-start.4 = (bf16[1024]{0:T(1024)(128)(2,1)S(1)}, bf16[1024]{0:T(1024)(128)(2,1)}, u32[]{:S(2)}) copy-start(bf16[1024]{0:T(1024)(128)(2,1)} %param.12) | copy-start | bytes 6148
  1.9 38.3 %all-to-all-start.1 = ((bf16[32,32,512]{2,1,0:T(8,128)(2,1)}), bf16[32,32,512]{2,1,0:T(8,128)(2,1)}, u32[]{:S(2)}, u32[]{:S(2)}) async-start(bf16[32,32,512]{2,1,0:T(8,128)(2,1)} %tile.5), calls=%async_computation.1 | async-start | bytes 2097152 | tf_op jit(solution)/shard_map/all_to_all | solution.py:29
  41.3 55.8 %all-to-all-start = ((bf16[32,32,512]{2,1,0:T(8,128)(2,1)}), bf16[32,32,512]{2,1,0:T(8,128)(2,1)}, u32[]{:S(2)}, u32[]{:S(2)}) async-start(bf16[32,32,512]{2,1,0:T(8,128)(2,1)} %tile.4), calls=%async_computation | async-start | bytes 2097152 | tf_op jit(solution)/shard_map/all_to_all | solution.py:29
  48.1 68.9 %collective-permute-start = (bf16[2,2,256,1024]{3,2,1,0:T(8,128)(2,1)S(1)}, bf16[2,2,256,1024]{3,2,1,0:T(8,128)(2,1)}, u32[]{:S(2)}, u32[]{:S(2)}) collective-permute-start(bf16[2,2,256,1024]{3,2,1,0:T(8,128)(2,1)S(1)} %copy-done.1), channel_id=1, source_target_pairs={{0,32},{32,64},{64,96},{96,128},{128,160},{160,192},{192,224},{224... | collective-permute-start | bytes 6291464 | tf_op jit(solution)/shard_map/ppermute | solution.py:18
  50.1 68.9 %collective-permute-start.1 = (bf16[2,2,256,1024]{3,2,1,0:T(8,128)(2,1)S(1)}, bf16[2,2,256,1024]{3,2,1,0:T(8,128)(2,1)}, u32[]{:S(2)}, u32[]{:S(2)}) collective-permute-start(bf16[2,2,256,1024]{3,2,1,0:T(8,128)(2,1)S(1)} %copy-done.1), channel_id=1, source_target_pairs={{32,0},{64,32},{96,64},{128,96},{160,128},{192,160},{224,192},{256... | collective-permute-start | bytes 6291464 | tf_op jit(solution)/shard_map/ppermute | solution.py:19
  60.0 71.0 %collective-permute-start.3 = (bf16[1024,512]{1,0:T(8,128)(2,1)}, bf16[1024,512]{1,0:T(8,128)(2,1)}, u32[]{:S(2)}, u32[]{:S(2)}) collective-permute-start(bf16[1024,512]{1,0:T(8,128)(2,1)} %bitcast.28), channel_id=1, source_target_pairs={{0,32},{32,0},{64,96},{96,64},{128,160},{160,128},{192,224},{224,1... | collective-permute-start | bytes 3145736 | tf_op jit(solution)/shard_map/ppermute | solution.py:32
  97.1 33.9 %collective-permute-start.2 = (bf16[1024,512]{1,0:T(8,128)(2,1)}, bf16[1024,512]{1,0:T(8,128)(2,1)}, u32[]{:S(2)}, u32[]{:S(2)}) collective-permute-start(bf16[1024,512]{1,0:T(8,128)(2,1)} %bitcast.22), channel_id=1, source_target_pairs={{0,32},{32,0},{64,96},{96,64},{128,160},{160,128},{192,224},{224,1... | collective-permute-start | bytes 3145736 | tf_op jit(solution)/shard_map/ppermute | solution.py:32
  131.0 3.5 %copy-start.3 = (bf16[256,1024]{1,0:T(8,128)(2,1)S(1)}, bf16[256,1024]{1,0:T(8,128)(2,1)}, u32[]{:S(2)}) copy-start(bf16[256,1024]{1,0:T(8,128)(2,1)} %param.11) | copy-start | bytes 1572868

commit v2 on v1

v2 whole, which is shorter than its diff:
```python
import jax
import jax.numpy as jnp
from jax import lax
from jax.experimental import pallas as pl
from jax.experimental.pallas import tpu as pltpu
from jax.sharding import PartitionSpec as P

H = 16
HD = 64
BLOCK_TOKENS = 256


def attention_kernel(slots_ref, count_ref, q_ref, *refs):
    key_refs, value_refs, out_ref = refs[: (len(refs) - 1) // 2], refs[(len(refs) - 1) // 2 : -1], refs[-1]
    count = count_ref[0]
    width = q_ref.shape[1]
    lane = lax.broadcasted_iota(jnp.int32, (1, width), 1)
    q_all = q_ref[...]
    result = None
    for head in range(width // HD):
        in_head = (lane >= head * HD) & (lane < (head + 1) * HD)
        q_head = jnp.where(in_head, q_all, jnp.zeros_like(q_all))
        scores = []
        for slot, key_ref in enumerate(key_refs):
            s = lax.dot_general(q_head, key_ref[...], (((1,), (1,)), ((), ())), preferred_element_type=jnp.float32)
            scores.append(jnp.where(slot < count, s, -jnp.inf))
        peak = scores[0].max(axis=1, keepdims=True)
        for s in scores[1:]:
            peak = jnp.maximum(peak, s.max(axis=1, keepdims=True))
        total = None
        mixed = None
        for s, value_ref in zip(scores, value_refs):
            expo = jnp.exp(s - peak)
            part = expo.sum(axis=1, keepdims=True)
            total = part if total is None else total + part
            term = jnp.dot(expo.astype(jnp.bfloat16), value_ref[...], preferred_element_type=jnp.float32)
            mixed = term if mixed is None else mixed + term
        head_out = mixed / total
        result = head_out if result is None else jnp.where(in_head, head_out, result)
    out_ref[...] = result.astype(out_ref.dtype)


def attend(q, window, slots, count, lanes=128):
    rows, width = q.shape
    nbr = slots.shape[0]
    q_spec = pl.BlockSpec((rows, lanes), lambda h, s, c: (0, h))
    def kv_spec(part, slot):
        return pl.BlockSpec((None, None, rows, lanes), lambda h, s, c: (part, s[slot], 0, h))
    in_specs = [q_spec] + [kv_spec(0, j) for j in range(nbr)] + [kv_spec(1, j) for j in range(nbr)]
    return pl.pallas_call(
        attention_kernel,
        grid_spec=pltpu.PrefetchScalarGridSpec(
            num_scalar_prefetch=2, grid=(width // lanes,), in_specs=in_specs, out_specs=q_spec),
        out_shape=jax.ShapeDtypeStruct((rows, width), jnp.bfloat16),
    )(slots, count, q, *([window] * (2 * nbr)))


def padded(array, sides, width):
    for axis, dim in sides:
        devices, length = (lax.axis_size(axis), array.shape[dim])
        up = [(i, (i + 1) % devices) for i in range(devices - 1)]
        down = [(j, i) for i, j in up]
        last = lax.slice_in_dim(array, length - width, length, axis=dim)
        initial = lax.slice_in_dim(array, 0, width, axis=dim)
        before = lax.ppermute(last, axis, up)
        after = lax.ppermute(initial, axis, down)
        array = jnp.concatenate([before, array, after], axis=dim)
    return array


def gathered_rows(local):
    lon_count = lax.axis_size("lon")
    core = lax.axis_index("lat") % 2
    half = local.shape[1] // 2
    mine = lax.dynamic_slice_in_dim(local, core * half, half, axis=1)
    fetched = lax.all_to_all(jnp.tile(mine, (lon_count, 1)), "lon", 0, 0, tiled=True)
    lat_count = lax.axis_size("lat")
    swap = [(i, i ^ 1) for i in range(lat_count)]
    other = lax.ppermute(fetched, "lat", swap)
    low = jnp.where(core == 0, fetched, other)
    high = jnp.where(core == 0, other, fetched)
    return jnp.concatenate([low, high], axis=1)


def on_device(queries, gain, w_query, w_out, kv_cache, nbr_lists, counts):
    rows = queries.astype(jnp.float32)
    rowwise_scale = lax.rsqrt(jnp.mean(rows * rows, axis=1, keepdims=True) + 1e-05)
    normed = (rows * rowwise_scale * gain.astype(jnp.float32)[None, :]).astype(jnp.bfloat16)
    projected = jnp.dot(
        normed,
        gathered_rows(w_query),
        preferred_element_type=jnp.float32,
    )
    query = (projected * HD ** (-0.5)).astype(jnp.bfloat16)
    blocks_here = kv_cache.shape[1]
    window = padded(kv_cache, (("lat", 1),), blocks_here)
    local_lists = nbr_lists - (lax.axis_index("lat") - 1) * blocks_here
    slots = jnp.clip(local_lists[0], 0, window.shape[1] - 1)
    attended = attend(query, window, slots, counts)
    decoded = lax.dot_general(
        attended,
        gathered_rows(w_out.T),
        (((1,), (1,)), ((), ())),
        preferred_element_type=jnp.float32,
    )
    return decoded.astype(jnp.bfloat16)


def solution(mesh):
    placed = (
        P(("lat", "lon"), None),
        P(),
        P("lon", None),
        P(None, "lon"),
        P(None, "lat", None, None),
        P(("lat", "lon"), None),
        P(("lat", "lon")),
    )
    return jax.shard_map(
        on_device, mesh=mesh, in_specs=placed, out_specs=P(("lat", "lon"), None), check_vma=False
    )
```

time: 175 us -> 143 us (0.82)
  the two profiles are of different devices: /device:TPU:176 before, /device:TPU:15 now
where the time goes in v2:
time: 143 us; the launch traced here: 142 us
  waiting for transfers between devices  79.4 us (56%)
  starting transfers between devices  33.3 us (23%)
  Pallas kernels  12.3 us (9%)
  other arithmetic  8.81 us (6%)
  local copies, waits for them, and re-layouts  3.9 us (3%)
  matrix products  3.08 us (2%)
    all_to_all x2, waiting for transfers between devices, gathered_rows(): lax.all_to_all(jnp.tile(mine, (lon_count, 1)), 'lon', 0, 0, tiled=True)  65.1 us
    all_to_all x2, starting transfers between devices, gathered_rows(): lax.all_to_all(jnp.tile(mine, (lon_count, 1)), 'lon', 0, 0, tiled=True)  19.7 us
    pallas_call x1, Pallas kernels, attend(): pl.pallas_call(attention_kernel, grid_spec=pltpu.PrefetchScalarGridSpec(n...  12.3 us
    ppermute x1, waiting for transfers between devices, padded(): before = lax.ppermute(last, axis, up)  10.7 us
    concatenate x1, other arithmetic, padded(): array = jnp.concatenate([before, array, after], axis=dim)  6.39 us
    ppermute x1, starting transfers between devices, padded(): before = lax.ppermute(last, axis, up)  6.25 us
    ppermute x2, starting transfers between devices, gathered_rows(): other = lax.ppermute(fetched, 'lat', swap)  5.48 us
    ppermute x1, waiting for transfers between devices, padded(): after = lax.ppermute(initial, axis, down)  3.64 us
  transfers between devices with their start and end apart: 6, of which 4 were waited for; matrix products, arithmetic and copies ran while one was open for 7% of the time, Pallas kernels for 9%

profile of v2, /device:TPU:15, one launch (start us, length us, event | category | flops | bytes accessed | tf_op | source)
XLA Modules:
  0.0 141.7 jit_solution(6716610915018598779)
XLA Ops:
  0.0 0.0 copy-start
  0.0 0.0 copy-start.4
  0.0 0.8 copy-done
  0.8 1.1 tile.4
  1.9 13.4 %all-to-all-start = ((bf16[32,32,512]{2,1,0:T(8,128)(2,1)}), bf16[32,32,512]{2,1,0:T(8,128)(2,1)S(1)}, u32[]{:S(2)}, u32[]{:S(2)}) async-start(bf16[32,32,512]{2,1,0:T(8,128)(2,1)} %tile.4), calls=%async_computation | async-start | bytes 2097152 | tf_op jit(solution)/shard_map/all_to_all | solution.py:76
  15.4 0.0 copy-done.4
  15.4 0.0 copy-start.2
  15.4 0.0 copy-start.6
  15.4 0.0 copy-start.5
  15.4 27.0 %all-to-all-done = bf16[32,32,512]{2,1,0:T(8,128)(2,1)S(1)} async-done(((bf16[32,32,512]{2,1,0:T(8,128)(2,1)}), bf16[32,32,512]{2,1,0:T(8,128)(2,1)S(1)}, u32[]{:S(2)}, u32[]{:S(2)}) %all-to-all-start) | async-done | bytes 1048608 | tf_op jit(solution)/shard_map/all_to_all | solution.py:76
  42.4 1.1 tile.5
  43.5 6.3 %all-to-all-start.1 = ((bf16[32,32,512]{2,1,0:T(8,128)(2,1)}), bf16[32,32,512]{2,1,0:T(8,128)(2,1)S(1)}, u32[]{:S(2)}, u32[]{:S(2)}) async-start(bf16[32,32,512]{2,1,0:T(8,128)(2,1)} %tile.5), calls=%async_computation.1 | async-start | bytes 2097152 | tf_op jit(solution)/shard_map/all_to_all | solution.py:76
  49.8 6.3 %collective-permute-start.1 = (bf16[2,2,256,1024]{3,2,1,0:T(8,128)(2,1)}, bf16[2,2,256,1024]{3,2,1,0:T(8,128)(2,1)}, u32[]{:S(2)}, u32[]{:S(2)}) collective-permute-start(bf16[2,2,256,1024]{3,2,1,0:T(8,128)(2,1)} %param.11), channel_id=1, source_target_pairs={{0,32},{32,64},{64,96},{96,128},{128,160},{160,192},{192,224},{224... | collective-permute-start | bytes 6291464 | tf_op jit(solution)/shard_map/ppermute | solution.py:65
  56.1 1.9 %collective-permute-start.2 = (bf16[2,2,256,1024]{3,2,1,0:T(8,128)(2,1)}, bf16[2,2,256,1024]{3,2,1,0:T(8,128)(2,1)}, u32[]{:S(2)}, u32[]{:S(2)}) collective-permute-start(bf16[2,2,256,1024]{3,2,1,0:T(8,128)(2,1)} %param.11), channel_id=1, source_target_pairs={{32,0},{64,32},{96,64},{128,96},{160,128},{192,160},{224,192},{256... | collective-permute-start | bytes 6291464 | tf_op jit(solution)/shard_map/ppermute | solution.py:66
  58.0 1.9 %collective-permute-start = (bf16[1024,512]{1,0:T(8,128)(2,1)S(1)}, bf16[1024,512]{1,0:T(8,128)(2,1)}, u32[]{:S(2)}, u32[]{:S(2)}) collective-permute-start(bf16[1024,512]{1,0:T(8,128)(2,1)S(1)} %bitcast.12), channel_id=1, source_target_pairs={{0,32},{32,0},{64,96},{96,64},{128,160},{160,128},{192,224},{224,1... | collective-permute-start | bytes 3145736 | tf_op jit(solution)/shard_map/ppermute | solution.py:79
  59.9 0.0 copy-done.2
  60.0 0.2 fusion.17
  60.1 38.1 %all-to-all-done.1 = bf16[32,32,512]{2,1,0:T(8,128)(2,1)S(1)} async-done(((bf16[32,32,512]{2,1,0:T(8,128)(2,1)}), bf16[32,32,512]{2,1,0:T(8,128)(2,1)S(1)}, u32[]{:S(2)}, u32[]{:S(2)}) %all-to-all-start.1) | async-done | bytes 1048608 | tf_op jit(solution)/shard_map/all_to_all | solution.py:76
  98.2 3.6 %collective-permute-start.3 = (bf16[1024,512]{1,0:T(8,128)(2,1)S(1)}, bf16[1024,512]{1,0:T(8,128)(2,1)S(1)}, u32[]{:S(2)}, u32[]{:S(2)}) collective-permute-start(bf16[1024,512]{1,0:T(8,128)(2,1)S(1)} %bitcast.11), channel_id=1, source_target_pairs={{0,32},{32,0},{64,96},{96,64},{128,160},{160,128},{192,224},{224,1... | collective-permute-start | bytes 3145736 | tf_op jit(solution)/shard_map/ppermute | solution.py:79
  101.8 0.0 copy-done.6
  101.8 0.6 clamp_bitcast_fusion.slots_ref
  102.4 0.0 copy-done.5
  103.0 10.7 %collective-permute-done.1 = bf16[2,2,256,1024]{3,2,1,0:T(8,128)(2,1)} collective-permute-done((bf16[2,2,256,1024]{3,2,1,0:T(8,128)(2,1)}, bf16[2,2,256,1024]{3,2,1,0:T(8,128)(2,1)}, u32[]{:S(2)}, u32[]{:S(2)}) %collective-permute-start.1) | collective-permute-done | bytes 2097184 | tf_op jit(solution)/shard_map/ppermute | solution.py:65
  113.8 3.6 %collective-permute-done.2 = bf16[2,2,256,1024]{3,2,1,0:T(8,128)(2,1)} collective-permute-done((bf16[2,2,256,1024]{3,2,1,0:T(8,128)(2,1)}, bf16[2,2,256,1024]{3,2,1,0:T(8,128)(2,1)}, u32[]{:S(2)}, u32[]{:S(2)}) %collective-permute-start.2) | collective-permute-done | bytes 2097184 | tf_op jit(solution)/shard_map/ppermute | solution.py:66
  117.4 6.4 %pad_maximum_fusion.refs_0_.refs_1_.refs_2_.refs_3_.refs_4_.refs_5_.refs_6_.refs_7_ = bf16[2,6,256,1024]{3,2,1,0:T(8,128)(2,1)} fusion(bf16[2,2,256,1024]{3,2,1,0:T(8,128)(2,1)} %collective-permute-done.2, bf16[2,2,256,1024]{3,2,1,0:T(8,128)(2,1)} %param.11, bf16[2,2,256,1024]{3,2,1,0:T(8,128)(2,1)} %collective-permute-done.1), kind=kLoop, calls=%fused_computation | loop fusion | flops 6291456 | bytes 12582912 | tf_op jit(solution)/shard_map/concatenate | solution.py:67
  123.8 0.0 copy-start.3
  123.8 0.0 collective-permute-done
  123.8 1.4 %broadcast_select_fusion.3 = (bf16[1024,512]{1,0:T(8,128)(2,1)S(1)}, bf16[1024,512]{1,0:T(8,128)(2,1)S(1)}) fusion(bf16[1024,512]{1,0:T(8,128)(2,1)} %collective-permute-done, pred[]{:T(512)S(6)} %eq.5, bf16[32,32,512]{2,1,0:T(8,128)(2,1)S(1)} %all-to-all-done), kind=kLoop, calls=%fused_computation.20 | loop fusion | flops 1048576 | bytes 4194305 | tf_op jit(solution)/shard_map/jit(_where)/select_n | solution.py:80
  125.2 0.0 copy-done.3
  125.2 1.5 %fusion.11.q_ref = bf16[256,1024]{1,0:T(8,128)(2,1)} fusion(bf16[1024,512]{1,0:T(8,128)(2,1)S(1)} %get-tuple-element.8, bf16[1024,512]{1,0:T(8,128)(2,1)S(1)} %get-tuple-element.7, bf16[256,1024]{1,0:T(8,128)(2,1)S(1)} %copy-done.3, f32[1024]{0:T(1024)S(1)} %convert_element_type.16, f32[256]{0:T(256)S(1)} %add_rsqrt_fusion), kind=kOutput, calls=%fused_computation.12 | convolution fusion | flops 542638080 | bytes 3150848 | tf_op jit(solution)/shard_map/dot_general | solution.py:89
  126.8 12.3 %shard_map.73 = bf16[256,1024]{1,0:T(8,128)(2,1)} custom-call(s32[4]{0:T(128)} %clamp_bitcast_fusion.slots_ref, s32[1]{0:T(128)S(6)} %copy.8.count_ref, bf16[256,1024]{1,0:T(8,128)(2,1)} %fusion.11.q_ref, bf16[2,6,256,1024]{3,2,1,0:T(8,128)(2,1)} %pad_maximum_fusion.refs_0_.refs_1_.refs_2_.refs_3_.refs_4_.refs_5_.refs_6_.refs_7_, ...), custom_call_target="tpu_custom_call" | custom-call | tf_op jit(solution)/shard_map/pallas_call | solution.py:50
  139.1 0.0 copy-start.1
  139.1 0.0 collective-permute-done.3
  139.1 0.2 broadcast_select_fusion.1
  139.3 0.8 copy-done.1
  140.1 1.5 %fusion.14 = bf16[256,1024]{1,0:T(8,128)(2,1)} fusion(bf16[256,1024]{1,0:T(8,128)(2,1)S(1)} %copy-done.1, bf16[1024,512]{1,0:T(8,128)(2,1)S(1)} %get-tuple-element.6, bf16[1024,512]{1,0:T(8,128)(2,1)S(1)} %get-tuple-element.5), kind=kOutput, calls=%fused_computation.13 | convolution fusion | flops 541327360 | bytes 3145728 | tf_op jit(solution)/shard_map/dot_general | solution.py:100
  (4 shorter events, 0.0 us)
Async XLA Ops:
  0.0 0.8 copy-start
  0.0 15.4 %copy-start.4 = (bf16[1024,32]{0,1:T(8,128)(2,1)S(1)}, bf16[1024,32]{0,1:T(8,128)(2,1)}, u32[]{:S(2)}) copy-start(bf16[1024,32]{0,1:T(8,128)(2,1)} %param.10) | copy-start | bytes 196612
  1.9 40.5 %all-to-all-start = ((bf16[32,32,512]{2,1,0:T(8,128)(2,1)}), bf16[32,32,512]{2,1,0:T(8,128)(2,1)S(1)}, u32[]{:S(2)}, u32[]{:S(2)}) async-start(bf16[32,32,512]{2,1,0:T(8,128)(2,1)} %tile.4), calls=%async_computation | async-start | bytes 2097152 | tf_op jit(solution)/shard_map/all_to_all | solution.py:76
  15.4 44.6 %copy-start.2 = (bf16[256,1024]{1,0:T(8,128)(2,1)S(1)}, bf16[256,1024]{1,0:T(8,128)(2,1)}, u32[]{:S(2)}) copy-start(bf16[256,1024]{1,0:T(8,128)(2,1)} %param.7) | copy-start | bytes 1572868
  15.4 86.4 %copy-start.6 = (s32[1,4]{1,0:T(1,128)S(1)}, s32[1,4]{1,0:T(1,128)}, u32[]{:S(2)}) copy-start(s32[1,4]{1,0:T(1,128)} %param.12) | copy-start | bytes 52
  15.4 87.0 %copy-start.5 = (bf16[1024]{0:T(1024)(128)(2,1)S(1)}, bf16[1024]{0:T(1024)(128)(2,1)}, u32[]{:S(2)}) copy-start(bf16[1024]{0:T(1024)(128)(2,1)} %param.8) | copy-start | bytes 6148
  43.5 54.7 %all-to-all-start.1 = ((bf16[32,32,512]{2,1,0:T(8,128)(2,1)}), bf16[32,32,512]{2,1,0:T(8,128)(2,1)S(1)}, u32[]{:S(2)}, u32[]{:S(2)}) async-start(bf16[32,32,512]{2,1,0:T(8,128)(2,1)} %tile.5), calls=%async_computation.1 | async-start | bytes 2097152 | tf_op jit(solution)/shard_map/all_to_all | solution.py:76
  49.8 63.9 %collective-permute-start.1 = (bf16[2,2,256,1024]{3,2,1,0:T(8,128)(2,1)}, bf16[2,2,256,1024]{3,2,1,0:T(8,128)(2,1)}, u32[]{:S(2)}, u32[]{:S(2)}) collective-permute-start(bf16[2,2,256,1024]{3,2,1,0:T(8,128)(2,1)} %param.11), channel_id=1, source_target_pairs={{0,32},{32,64},{64,96},{96,128},{128,160},{160,192},{192,224},{224... | collective-permute-start | bytes 6291464 | tf_op jit(solution)/shard_map/ppermute | solution.py:65
  56.1 61.3 %collective-permute-start.2 = (bf16[2,2,256,1024]{3,2,1,0:T(8,128)(2,1)}, bf16[2,2,256,1024]{3,2,1,0:T(8,128)(2,1)}, u32[]{:S(2)}, u32[]{:S(2)}) collective-permute-start(bf16[2,2,256,1024]{3,2,1,0:T(8,128)(2,1)} %param.11), channel_id=1, source_target_pairs={{32,0},{64,32},{96,64},{128,96},{160,128},{192,160},{224,192},{256... | collective-permute-start | bytes 6291464 | tf_op jit(solution)/shard_map/ppermute | solution.py:66
  58.0 65.8 %collective-permute-start = (bf16[1024,512]{1,0:T(8,128)(2,1)S(1)}, bf16[1024,512]{1,0:T(8,128)(2,1)}, u32[]{:S(2)}, u32[]{:S(2)}) collective-permute-start(bf16[1024,512]{1,0:T(8,128)(2,1)S(1)} %bitcast.12), channel_id=1, source_target_pairs={{0,32},{32,0},{64,96},{96,64},{128,160},{160,128},{192,224},{224,1... | collective-permute-start | bytes 3145736 | tf_op jit(solution)/shard_map/ppermute | solution.py:79
  98.2 40.9 %collective-permute-start.3 = (bf16[1024,512]{1,0:T(8,128)(2,1)S(1)}, bf16[1024,512]{1,0:T(8,128)(2,1)S(1)}, u32[]{:S(2)}, u32[]{:S(2)}) collective-permute-start(bf16[1024,512]{1,0:T(8,128)(2,1)S(1)} %bitcast.11), channel_id=1, source_target_pairs={{0,32},{32,0},{64,96},{96,64},{128,160},{160,128},{192,224},{224,1... | collective-permute-start | bytes 3145736 | tf_op jit(solution)/shard_map/ppermute | solution.py:79
  123.8 1.4 %copy-start.3 = (bf16[256,1024]{1,0:T(8,128)(2,1)S(1)}, bf16[256,1024]{1,0:T(8,128)(2,1)}, u32[]{:S(2)}) copy-start(bf16[256,1024]{1,0:T(8,128)(2,1)} %param.7) | copy-start | bytes 1572868
  139.1 1.0 copy-start.1

commit v3 on v2

--- a/solution.py
+++ b/solution.py
@@ -5,9 +5,8 @@
 from jax.experimental.pallas import tpu as pltpu
 from jax.sharding import PartitionSpec as P
 
-H = 16
+
 HD = 64
-BLOCK_TOKENS = 256
 
 
 def attention_kernel(slots_ref, count_ref, q_ref, *refs):
@@ -68,11 +67,13 @@
     return array
 
 
-def gathered_rows(local):
+def gathered_rows(local, after=None):
     lon_count = lax.axis_size("lon")
     core = lax.axis_index("lat") % 2
     half = local.shape[1] // 2
     mine = lax.dynamic_slice_in_dim(local, core * half, half, axis=1)
+    if after is not None:
+        mine, _ = lax.optimization_barrier((mine, after))
     fetched = lax.all_to_all(jnp.tile(mine, (lon_count, 1)), "lon", 0, 0, tiled=True)
     lat_count = lax.axis_size("lat")
     swap = [(i, i ^ 1) for i in range(lat_count)]
@@ -82,7 +83,7 @@
     return jnp.concatenate([low, high], axis=1)
 
 
-def on_device(queries, gain, w_query, w_out, kv_cache, nbr_lists, counts):
+def layer(queries, gain, w_query, w_out, kv_cache, nbr_lists, counts):
     rows = queries.astype(jnp.float32)
     rowwise_scale = lax.rsqrt(jnp.mean(rows * rows, axis=1, keepdims=True) + 1e-05)
     normed = (rows * rowwise_scale * gain.astype(jnp.float32)[None, :]).astype(jnp.bfloat16)
@@ -97,9 +98,10 @@
     local_lists = nbr_lists - (lax.axis_index("lat") - 1) * blocks_here
     slots = jnp.clip(local_lists[0], 0, window.shape[1] - 1)
     attended = attend(query, window, slots, counts)
+    w_out_rows = gathered_rows(w_out.T, after=query)
     decoded = lax.dot_general(
         attended,
-        gathered_rows(w_out.T),
+        w_out_rows,
         (((1,), (1,)), ((), ())),
         preferred_element_type=jnp.float32,
     )
@@ -116,6 +118,4 @@
         P(("lat", "lon"), None),
         P(("lat", "lon")),
     )
-    return jax.shard_map(
-        on_device, mesh=mesh, in_specs=placed, out_specs=P(("lat", "lon"), None), check_vma=False
-    )
+    return jax.shard_map(layer, mesh=mesh, in_specs=placed, out_specs=P(("lat", "lon"), None), check_vma=False)

time: 143 us -> 146 us (1.021)
  the two profiles are of different devices: /device:TPU:15 before, /device:TPU:48 now
where the time goes in v3:
time: 146 us; the launch traced here: 145 us
  waiting for transfers between devices  57.4 us (39%)
  blocking collectives  40.3 us (28%)
  starting transfers between devices  21.7 us (15%)
  Pallas kernels  12.2 us (8%)
  other arithmetic  7.83 us (5%)
  matrix products  3.1 us (2%)
  local copies, waits for them, and re-layouts  2.04 us (1%)
    all_to_all x1, blocking collectives, gathered_rows(): lax.all_to_all(jnp.tile(mine, (lon_count, 1)), 'lon', 0, 0, tiled=True)  40.3 us
    all_to_all x1, waiting for transfers between devices, gathered_rows(): lax.all_to_all(jnp.tile(mine, (lon_count, 1)), 'lon', 0, 0, tiled=True)  37.6 us
    ppermute x1, waiting for transfers between devices, padded(): before = lax.ppermute(last, axis, up)  17.4 us
    pallas_call x1, Pallas kernels, attend(): pl.pallas_call(attention_kernel, grid_spec=pltpu.PrefetchScalarGridSpec(n...  12.2 us
    ppermute x1, starting transfers between devices, padded(): after = lax.ppermute(initial, axis, down)  9.66 us
    all_to_all x1, starting transfers between devices, gathered_rows(): lax.all_to_all(jnp.tile(mine, (lon_count, 1)), 'lon', 0, 0, tiled=True)  6.29 us
    concatenate x1, other arithmetic, padded(): array = jnp.concatenate([before, array, after], axis=dim)  5.43 us
    ppermute x2, starting transfers between devices, gathered_rows(): other = lax.ppermute(fetched, 'lat', swap)  3.82 us
  transfers between devices with their start and end apart: 5, of which 3 were waited for; matrix products, arithmetic and copies ran while one was open for 4% of the time, Pallas kernels for 8%

profile of v3, /device:TPU:48, one launch (start us, length us, event | category | flops | bytes accessed | tf_op | source)
XLA Modules:
  0.0 145.3 jit_solution(5200416684547814021)
XLA Ops:
  0.0 0.0 copy-start
  0.0 0.0 copy-start.5
  0.0 0.0 copy-start.4
  0.0 0.0 copy-start.3
  0.0 0.8 copy-done
  0.8 0.1 tile.4
  1.0 40.3 %all_to_all.18 = bf16[32,32,512]{2,1,0:T(8,128)(2,1)S(1)} all-to-all(bf16[32,32,512]{2,1,0:T(8,128)(2,1)S(1)} %tile.4), channel_id=1, replica_groups=mesh['lat'=16,'lon'=32] {'lon'}, dimensions={0} | all-to-all | bytes 2097152 | tf_op jit(solution)/shard_map/all_to_all | solution.py:77
  41.2 1.9 %collective-permute-start = (bf16[1024,512]{1,0:T(8,128)(2,1)S(1)}, bf16[1024,512]{1,0:T(8,128)(2,1)S(1)}, u32[]{:S(2)}, u32[]{:S(2)}) collective-permute-start(bf16[1024,512]{1,0:T(8,128)(2,1)S(1)} %bitcast.12), channel_id=1, source_target_pairs={{0,32},{32,0},{64,96},{96,64},{128,160},{160,128},{192,224},{224,1... | collective-permute-start | bytes 3145736 | tf_op jit(solution)/shard_map/ppermute | solution.py:80
  43.1 0.0 copy-done.5
  43.2 0.0 copy-done.4
  43.2 0.0 copy-done.3
  43.2 0.2 fusion.17
  43.4 2.4 %collective-permute-done = bf16[1024,512]{1,0:T(8,128)(2,1)S(1)} collective-permute-done((bf16[1024,512]{1,0:T(8,128)(2,1)S(1)}, bf16[1024,512]{1,0:T(8,128)(2,1)S(1)}, u32[]{:S(2)}, u32[]{:S(2)}) %collective-permute-start) | collective-permute-done | bytes 1048608 | tf_op jit(solution)/shard_map/ppermute | solution.py:80
  45.8 0.2 broadcast_select_fusion.3
  46.0 1.6 %fusion.11.q_ref = bf16[256,1024]{1,0:T(8,128)(2,1)} fusion(bf16[1024,512]{1,0:T(8,128)(2,1)S(1)} %get-tuple-element.10, bf16[1024,512]{1,0:T(8,128)(2,1)S(1)} %get-tuple-element.9, bf16[256,1024]{1,0:T(8,128)(2,1)S(1)} %copy-done.3, f32[1024]{0:T(1024)S(1)} %convert_element_type.16, f32[256]{0:T(256)S(1)} %add_rsqrt_fusion), kind=kOutput, calls=%fused_computation.12 | convolution fusion | flops 542638080 | bytes 3150848 | tf_op jit(solution)/shard_map/dot_general | solution.py:90
  47.5 0.0 copy-start.1
  47.5 0.0 copy-start.6
  47.5 1.1 tile.5
  48.6 6.3 %all-to-all-start.1 = ((bf16[32,32,512]{2,1,0:T(8,128)(2,1)}), bf16[32,32,512]{2,1,0:T(8,128)(2,1)S(1)}, u32[]{:S(2)}, u32[]{:S(2)}) async-start(bf16[32,32,512]{2,1,0:T(8,128)(2,1)} %tile.5), calls=%async_computation.1 | async-start | bytes 2097152 | tf_op jit(solution)/shard_map/all_to_all | solution.py:77
  54.9 0.0 copy-done.1
  54.9 1.9 %collective-permute-start.1 = (bf16[2,2,256,1024]{3,2,1,0:T(8,128)(2,1)S(1)}, bf16[2,2,256,1024]{3,2,1,0:T(8,128)(2,1)}, u32[]{:S(2)}, u32[]{:S(2)}) collective-permute-start(bf16[2,2,256,1024]{3,2,1,0:T(8,128)(2,1)S(1)} %copy-done.1), channel_id=1, source_target_pairs={{0,32},{32,64},{64,96},{96,128},{128,160},{160,192},{192,224},{224... | collective-permute-start | bytes 6291464 | tf_op jit(solution)/shard_map/ppermute | solution.py:64
  56.9 9.7 %collective-permute-start.2 = (bf16[2,2,256,1024]{3,2,1,0:T(8,128)(2,1)S(1)}, bf16[2,2,256,1024]{3,2,1,0:T(8,128)(2,1)}, u32[]{:S(2)}, u32[]{:S(2)}) collective-permute-start(bf16[2,2,256,1024]{3,2,1,0:T(8,128)(2,1)S(1)} %copy-done.1), channel_id=1, source_target_pairs={{32,0},{64,32},{96,64},{128,96},{160,128},{192,160},{224,192},{256... | collective-permute-start | bytes 6291464 | tf_op jit(solution)/shard_map/ppermute | solution.py:65
  66.5 37.6 %all-to-all-done.1 = bf16[32,32,512]{2,1,0:T(8,128)(2,1)S(1)} async-done(((bf16[32,32,512]{2,1,0:T(8,128)(2,1)}), bf16[32,32,512]{2,1,0:T(8,128)(2,1)S(1)}, u32[]{:S(2)}, u32[]{:S(2)}) %all-to-all-start.1) | async-done | bytes 1048608 | tf_op jit(solution)/shard_map/all_to_all | solution.py:77
  104.1 1.9 %collective-permute-start.3 = (bf16[1024,512]{1,0:T(8,128)(2,1)S(1)}, bf16[1024,512]{1,0:T(8,128)(2,1)}, u32[]{:S(2)}, u32[]{:S(2)}) collective-permute-start(bf16[1024,512]{1,0:T(8,128)(2,1)S(1)} %bitcast.11), channel_id=1, source_target_pairs={{0,32},{32,0},{64,96},{96,64},{128,160},{160,128},{192,224},{224,1... | collective-permute-start | bytes 3145736 | tf_op jit(solution)/shard_map/ppermute | solution.py:80
  106.7 0.0 copy-done.6
  106.7 0.6 clamp_bitcast_fusion.slots_ref
  107.3 17.4 %collective-permute-done.1 = bf16[2,2,256,1024]{3,2,1,0:T(8,128)(2,1)} collective-permute-done((bf16[2,2,256,1024]{3,2,1,0:T(8,128)(2,1)S(1)}, bf16[2,2,256,1024]{3,2,1,0:T(8,128)(2,1)}, u32[]{:S(2)}, u32[]{:S(2)}) %collective-permute-start.1) | collective-permute-done | bytes 2097184 | tf_op jit(solution)/shard_map/ppermute | solution.py:64
  124.7 0.0 collective-permute-done.2
  124.7 5.4 %pad_maximum_fusion.refs_0_.refs_1_.refs_2_.refs_3_.refs_4_.refs_5_.refs_6_.refs_7_ = bf16[2,6,256,1024]{3,2,1,0:T(8,128)(2,1)} fusion(bf16[2,2,256,1024]{3,2,1,0:T(8,128)(2,1)} %collective-permute-done.2, bf16[2,2,256,1024]{3,2,1,0:T(8,128)(2,1)S(1)} %copy-done.1, bf16[2,2,256,1024]{3,2,1,0:T(8,128)(2,1)} %collective-permute-done.1), kind=kLoop, calls=%fused_computation | loop fusion | flops 6291456 | bytes 12582912 | tf_op jit(solution)/shard_map/concatenate | solution.py:66
  130.1 12.2 %shard_map.73 = bf16[256,1024]{1,0:T(8,128)(2,1)} custom-call(s32[4]{0:T(128)} %clamp_bitcast_fusion.slots_ref, s32[1]{0:T(128)S(6)} %copy.8.count_ref, bf16[256,1024]{1,0:T(8,128)(2,1)} %fusion.11.q_ref, bf16[2,6,256,1024]{3,2,1,0:T(8,128)(2,1)} %pad_maximum_fusion.refs_0_.refs_1_.refs_2_.refs_3_.refs_4_.refs_5_.refs_6_.refs_7_, ...), custom_call_target="tpu_custom_call" | custom-call | tf_op jit(solution)/shard_map/pallas_call | solution.py:49
  142.3 0.0 copy-start.2
  142.3 0.0 collective-permute-done.3
  142.3 1.4 broadcast_select_fusion.1
  143.7 0.0 copy-done.2
  143.7 1.5 %fusion.14 = bf16[256,1024]{1,0:T(8,128)(2,1)} fusion(bf16[256,1024]{1,0:T(8,128)(2,1)S(1)} %copy-done.2, bf16[1024,512]{1,0:T(8,128)(2,1)S(1)} %get-tuple-element.8, bf16[1024,512]{1,0:T(8,128)(2,1)S(1)} %get-tuple-element.7), kind=kOutput, calls=%fused_computation.13 | convolution fusion | flops 541327360 | bytes 3145728 | tf_op jit(solution)/shard_map/dot_general | solution.py:102
  (4 shorter events, 0.0 us)
Async XLA Ops:
  0.0 0.8 copy-start
  0.0 43.1 %copy-start.5 = (bf16[1024]{0:T(1024)(128)(2,1)S(1)}, bf16[1024]{0:T(1024)(128)(2,1)}, u32[]{:S(2)}) copy-start(bf16[1024]{0:T(1024)(128)(2,1)} %param.8) | copy-start | bytes 6148
  0.0 43.2 %copy-start.4 = (bf16[1024,32]{0,1:T(8,128)(2,1)S(1)}, bf16[1024,32]{0,1:T(8,128)(2,1)}, u32[]{:S(2)}) copy-start(bf16[1024,32]{0,1:T(8,128)(2,1)} %param.10) | copy-start | bytes 196612
  0.0 43.2 %copy-start.3 = (bf16[256,1024]{1,0:T(8,128)(2,1)S(1)}, bf16[256,1024]{1,0:T(8,128)(2,1)}, u32[]{:S(2)}) copy-start(bf16[256,1024]{1,0:T(8,128)(2,1)} %param.7) | copy-start | bytes 1572868
  41.2 4.5 %collective-permute-start = (bf16[1024,512]{1,0:T(8,128)(2,1)S(1)}, bf16[1024,512]{1,0:T(8,128)(2,1)S(1)}, u32[]{:S(2)}, u32[]{:S(2)}) collective-permute-start(bf16[1024,512]{1,0:T(8,128)(2,1)S(1)} %bitcast.12), channel_id=1, source_target_pairs={{0,32},{32,0},{64,96},{96,64},{128,160},{160,128},{192,224},{224,1... | collective-permute-start | bytes 3145736 | tf_op jit(solution)/shard_map/ppermute | solution.py:80
  47.5 7.4 %copy-start.1 = (bf16[2,2,256,1024]{3,2,1,0:T(8,128)(2,1)S(1)}, bf16[2,2,256,1024]{3,2,1,0:T(8,128)(2,1)}, u32[]{:S(2)}) copy-start(bf16[2,2,256,1024]{3,2,1,0:T(8,128)(2,1)} %param.11) | copy-start | bytes 6291460
  47.5 59.2 %copy-start.6 = (s32[1,4]{1,0:T(1,128)S(1)}, s32[1,4]{1,0:T(1,128)}, u32[]{:S(2)}) copy-start(s32[1,4]{1,0:T(1,128)} %param.12) | copy-start | bytes 52
  48.6 55.5 %all-to-all-start.1 = ((bf16[32,32,512]{2,1,0:T(8,128)(2,1)}), bf16[32,32,512]{2,1,0:T(8,128)(2,1)S(1)}, u32[]{:S(2)}, u32[]{:S(2)}) async-start(bf16[32,32,512]{2,1,0:T(8,128)(2,1)} %tile.5), calls=%async_computation.1 | async-start | bytes 2097152 | tf_op jit(solution)/shard_map/all_to_all | solution.py:77
  54.9 69.7 %collective-permute-start.1 = (bf16[2,2,256,1024]{3,2,1,0:T(8,128)(2,1)S(1)}, bf16[2,2,256,1024]{3,2,1,0:T(8,128)(2,1)}, u32[]{:S(2)}, u32[]{:S(2)}) collective-permute-start(bf16[2,2,256,1024]{3,2,1,0:T(8,128)(2,1)S(1)} %copy-done.1), channel_id=1, source_target_pairs={{0,32},{32,64},{64,96},{96,128},{128,160},{160,192},{192,224},{224... | collective-permute-start | bytes 6291464 | tf_op jit(solution)/shard_map/ppermute | solution.py:64
  56.9 67.8 %collective-permute-start.2 = (bf16[2,2,256,1024]{3,2,1,0:T(8,128)(2,1)S(1)}, bf16[2,2,256,1024]{3,2,1,0:T(8,128)(2,1)}, u32[]{:S(2)}, u32[]{:S(2)}) collective-permute-start(bf16[2,2,256,1024]{3,2,1,0:T(8,128)(2,1)S(1)} %copy-done.1), channel_id=1, source_target_pairs={{32,0},{64,32},{96,64},{128,96},{160,128},{192,160},{224,192},{256... | collective-permute-start | bytes 6291464 | tf_op jit(solution)/shard_map/ppermute | solution.py:65
  104.1 38.1 %collective-permute-start.3 = (bf16[1024,512]{1,0:T(8,128)(2,1)S(1)}, bf16[1024,512]{1,0:T(8,128)(2,1)}, u32[]{:S(2)}, u32[]{:S(2)}) collective-permute-start(bf16[1024,512]{1,0:T(8,128)(2,1)S(1)} %bitcast.11), channel_id=1, source_target_pairs={{0,32},{32,0},{64,96},{96,64},{128,160},{160,128},{192,224},{224,1... | collective-permute-start | bytes 3145736 | tf_op jit(solution)/shard_map/ppermute | solution.py:80
  142.3 1.4 copy-start.2

commit v4 on v3

--- a/solution.py
+++ b/solution.py
@@ -54,17 +54,38 @@
     )(slots, count, q, *([window] * (2 * nbr)))
 
 
-def padded(array, sides, width):
-    for axis, dim in sides:
-        devices, length = (lax.axis_size(axis), array.shape[dim])
-        up = [(i, (i + 1) % devices) for i in range(devices - 1)]
-        down = [(j, i) for i, j in up]
-        last = lax.slice_in_dim(array, length - width, length, axis=dim)
-        initial = lax.slice_in_dim(array, 0, width, axis=dim)
-        before = lax.ppermute(last, axis, up)
-        after = lax.ppermute(initial, axis, down)
-        array = jnp.concatenate([before, array, after], axis=dim)
-    return array
+Y_LO = 4
+
+
+def neighbour_bands(kv):
+    lat_count, lon_count = lax.axis_size("lat"), lax.axis_size("lon")
+    lat, lon = lax.axis_index("lat"), lax.axis_index("lon")
+    both = ("lat", "lon")
+    split = lat_count // 2
+    up = [(k * lon_count + l, (k + 1) * lon_count + l) for k in range(lat_count - 1) if k != split - 1 for l in range(lon_count)]
+    below = lax.ppermute(kv, both, up)
+    above = lax.ppermute(kv, both, [(j, i) for i, j in up])
+    rows = kv.shape[2] // Y_LO
+    y_lo = lon % Y_LO
+    piece = lax.dynamic_slice_in_dim(kv, (Y_LO - 1 - y_lo) * rows, rows, axis=2)
+    cross = []
+    for l in range(lon_count):
+        mirror = l - l % Y_LO + (Y_LO - 1 - l % Y_LO)
+        cross.append(((split - 1) * lon_count + l, split * lon_count + mirror))
+        cross.append((split * lon_count + l, (split - 1) * lon_count + mirror))
+    pieces = [lax.ppermute(piece, both, cross)]
+    for shift in range(1, Y_LO):
+        ring = []
+        for band in (split - 1, split):
+            for l in range(lon_count):
+                ring.append((band * lon_count + l, band * lon_count + l - l % Y_LO + (l % Y_LO + shift) % Y_LO))
+        pieces.append(lax.ppermute(pieces[0], both, ring))
+    order = (y_lo - jnp.arange(Y_LO)) % Y_LO
+    joined = jnp.take(jnp.stack(pieces), order, axis=0)
+    joined = jnp.moveaxis(joined, 0, 2).reshape(kv.shape)
+    below = jnp.where(lat == split, joined, below)
+    above = jnp.where(lat == split - 1, joined, above)
+    return below, above
 
 
 def gathered_rows(local, after=None):
@@ -94,7 +115,8 @@
     )
     query = (projected * HD ** (-0.5)).astype(jnp.bfloat16)
     blocks_here = kv_cache.shape[1]
-    window = padded(kv_cache, (("lat", 1),), blocks_here)
+    below, above = neighbour_bands(kv_cache)
+    window = jnp.concatenate([below, kv_cache, above], axis=1)
     local_lists = nbr_lists - (lax.axis_index("lat") - 1) * blocks_here
     slots = jnp.clip(local_lists[0], 0, window.shape[1] - 1)
     attended = attend(query, window, slots, counts)

time: 146 us -> 144 us (0.986)
  the two profiles are of different devices: /device:TPU:48 before, /device:TPU:57 now
where the time goes in v4:
time: 144 us; the launch traced here: 143 us
  starting transfers between devices  55 us (38%)
  blocking collectives  40.2 us (28%)
  waiting for transfers between devices  14.3 us (10%)
  Pallas kernels  12 us (8%)
  other arithmetic  11.5 us (8%)
  local copies, waits for them, and re-layouts  5.68 us (4%)
  matrix products  3.1 us (2%)
    ppermute x2, starting transfers between devices, gathered_rows(): other = lax.ppermute(fetched, 'lat', swap)  40.5 us
    all_to_all x1, blocking collectives, gathered_rows(): lax.all_to_all(jnp.tile(mine, (lon_count, 1)), 'lon', 0, 0, tiled=True)  40.2 us
    all_to_all x1, waiting for transfers between devices, gathered_rows(): lax.all_to_all(jnp.tile(mine, (lon_count, 1)), 'lon', 0, 0, tiled=True)  12.3 us
    pallas_call x1, Pallas kernels, attend(): pl.pallas_call(attention_kernel, grid_spec=pltpu.PrefetchScalarGridSpec(n...  12 us
    all_to_all x1, starting transfers between devices, gathered_rows(): lax.all_to_all(jnp.tile(mine, (lon_count, 1)), 'lon', 0, 0, tiled=True)  5.77 us
    concatenate x1, other arithmetic, layer(): window = jnp.concatenate([below, kv_cache, above], axis=1)  4.6 us
    ppermute x1, starting transfers between devices, neighbour_bands(): below = lax.ppermute(kv, both, up)  3.96 us
  transfers between devices with their start and end apart: 9, of which 2 were waited for; matrix products, arithmetic and copies ran while one was open for 9% of the time, Pallas kernels for 8%

profile of v4, /device:TPU:57, one launch (start us, length us, event | category | flops | bytes accessed | tf_op | source)
XLA Modules:
  0.0 142.7 jit_solution(11031514965974345755)
XLA Ops:
  0.0 0.0 copy-start
  0.0 0.0 copy-start.4
  0.0 0.0 copy-start.3
  0.0 0.0 copy-start.2
  0.0 0.8 copy-done
  0.8 0.1 tile.4
  1.0 40.2 %all_to_all.18 = bf16[32,32,512]{2,1,0:T(8,128)(2,1)S(1)} all-to-all(bf16[32,32,512]{2,1,0:T(8,128)(2,1)S(1)} %tile.4), channel_id=1, replica_groups=mesh['lat'=16,'lon'=32] {'lon'}, dimensions={0} | all-to-all | bytes 2097152 | tf_op jit(solution)/shard_map/all_to_all | solution.py:98
  41.2 3.4 %collective-permute-start = (bf16[1024,512]{1,0:T(8,128)(2,1)S(1)}, bf16[1024,512]{1,0:T(8,128)(2,1)S(1)}, u32[]{:S(2)}, u32[]{:S(2)}) collective-permute-start(bf16[1024,512]{1,0:T(8,128)(2,1)S(1)} %bitcast.23), channel_id=1, source_target_pairs={{0,32},{32,0},{64,96},{96,64},{128,160},{160,128},{192,224},{224,1... | collective-permute-start | bytes 3145736 | tf_op jit(solution)/shard_map/ppermute | solution.py:101
  44.5 0.0 copy-done.4
  44.6 0.0 copy-done.3
  44.6 0.0 copy-done.2
  44.6 0.2 fusion.17
  44.8 2.0 %collective-permute-done = bf16[1024,512]{1,0:T(8,128)(2,1)S(1)} collective-permute-done((bf16[1024,512]{1,0:T(8,128)(2,1)S(1)}, bf16[1024,512]{1,0:T(8,128)(2,1)S(1)}, u32[]{:S(2)}, u32[]{:S(2)}) %collective-permute-start) | collective-permute-done | bytes 1048608 | tf_op jit(solution)/shard_map/ppermute | solution.py:101
  46.8 0.2 broadcast_select_fusion.3
  47.0 1.6 %fusion.11.q_ref = bf16[256,1024]{1,0:T(8,128)(2,1)} fusion(bf16[1024,512]{1,0:T(8,128)(2,1)S(1)} %get-tuple-element.12, bf16[1024,512]{1,0:T(8,128)(2,1)S(1)} %get-tuple-element.11, bf16[256,1024]{1,0:T(8,128)(2,1)S(1)} %copy-done.2, f32[1024]{0:T(1024)S(1)} %convert_element_type.16, f32[256]{0:T(256)S(1)} %add_rsqrt_fusion), kind=kOutput, calls=%fused_computation.17 | convolution fusion | flops 542638080 | bytes 3150848 | tf_op jit(solution)/shard_map/dot_general | solution.py:111
  48.6 0.0 copy-start.5
  48.6 1.1 tile.5
  49.7 5.8 %all-to-all-start.1 = ((bf16[32,32,512]{2,1,0:T(8,128)(2,1)}), bf16[32,32,512]{2,1,0:T(8,128)(2,1)S(1)}, u32[]{:S(2)}, u32[]{:S(2)}) async-start(bf16[32,32,512]{2,1,0:T(8,128)(2,1)} %tile.5), calls=%async_computation.1 | async-start | bytes 2097152 | tf_op jit(solution)/shard_map/all_to_all | solution.py:98
  55.5 4.0 %collective-permute-start.5 = (bf16[2,2,256,1024]{3,2,1,0:T(8,128)(2,1)}, bf16[2,2,256,1024]{3,2,1,0:T(8,128)(2,1)}, u32[]{:S(2)}, u32[]{:S(2)}) collective-permute-start(bf16[2,2,256,1024]{3,2,1,0:T(8,128)(2,1)} %param.11), channel_id=1, source_target_pairs={{0,32},{1,33},{2,34},{3,35},{4,36},{5,37},{6,38},{7,39},{8,40},{9,... | collective-permute-start | bytes 6291464 | tf_op jit(solution)/shard_map/ppermute | solution.py:66
  59.4 1.9 %collective-permute-start.6 = (bf16[2,2,256,1024]{3,2,1,0:T(8,128)(2,1)}, bf16[2,2,256,1024]{3,2,1,0:T(8,128)(2,1)}, u32[]{:S(2)}, u32[]{:S(2)}) collective-permute-start(bf16[2,2,256,1024]{3,2,1,0:T(8,128)(2,1)} %param.11), channel_id=1, source_target_pairs={{32,0},{33,1},{34,2},{35,3},{36,4},{37,5},{38,6},{39,7},{40,8},{41... | collective-permute-start | bytes 6291464 | tf_op jit(solution)/shard_map/ppermute | solution.py:67
  61.4 1.1 constant_dynamic-slice_fusion
  62.5 0.7 collective-permute-start.1
  63.8 0.0 collective-permute-done.1
  63.8 0.7 collective-permute-start.2
  64.6 0.7 collective-permute-start.3
  65.3 0.7 collective-permute-start.4
  66.0 0.0 copy-done.5
  66.0 0.5 clamp_bitcast_fusion.slots_ref
  66.5 0.0 collective-permute-done.2
  66.5 0.0 collective-permute-done.3
  66.5 0.0 collective-permute-done.4
  66.5 1.6 %pad_maximum_fusion.1 = bf16[4,2,2,64,1024]{4,3,2,1,0:T(8,128)(2,1)} fusion(bf16[1,2,2,64,1024]{4,3,2,1,0:T(8,128)(2,1)S(1)} %bitcast.27, bf16[1,2,2,64,1024]{4,3,2,1,0:T(8,128)(2,1)S(1)} %bitcast.26, bf16[1,2,2,64,1024]{4,3,2,1,0:T(8,128)(2,1)S(1)} %bitcast.25, bf16[1,2,2,64,1024]{4,3,2,1,0:T(8,128)(2,1)S(1)} %bitcast.24), kind=kLoop, calls=%fused_computation.6 | loop fusion | flops 3145728 | bytes 4194304 | tf_op jit(solution)/shard_map/stack | solution.py:84
  68.2 2.3 %gather_fusion = bf16[4,2,2,64,1024]{4,3,2,1,0:T(8,128)(2,1)S(1)} fusion(bf16[4,2,2,64,1024]{4,3,2,1,0:T(8,128)(2,1)} %pad_maximum_fusion.1, s32[1024]{0:T(1024)S(1)} %pad_clamp_fusion), kind=kCustom, calls=%fused_computation | custom fusion | bytes 4194320 | tf_op jit(solution)/shard_map/jit(_take)/gather | solution.py:84
  70.4 12.3 %all-to-all-done.1 = bf16[32,32,512]{2,1,0:T(8,128)(2,1)S(1)} async-done(((bf16[32,32,512]{2,1,0:T(8,128)(2,1)}), bf16[32,32,512]{2,1,0:T(8,128)(2,1)S(1)}, u32[]{:S(2)}, u32[]{:S(2)}) %all-to-all-start.1) | async-done | bytes 1048608 | tf_op jit(solution)/shard_map/all_to_all | solution.py:98
  82.7 37.2 %collective-permute-start.7 = (bf16[1024,512]{1,0:T(8,128)(2,1)S(1)}, bf16[1024,512]{1,0:T(8,128)(2,1)}, u32[]{:S(2)}, u32[]{:S(2)}) collective-permute-start(bf16[1024,512]{1,0:T(8,128)(2,1)S(1)} %bitcast.22), channel_id=1, source_target_pairs={{0,32},{32,0},{64,96},{96,64},{128,160},{160,128},{192,224},{224,1... | collective-permute-start | bytes 3145736 | tf_op jit(solution)/shard_map/ppermute | solution.py:101
  119.9 0.3 select_bitcast_fusion
  120.2 0.3 copy.8
  120.4 0.0 collective-permute-done.5
  120.4 0.0 collective-permute-done.6
  120.5 2.6 %bitcast_select_fusion.1 = (bf16[2,2,256,1024]{3,2,1,0:T(8,128)(2,1)S(1)}, bf16[2,2,256,1024]{3,2,1,0:T(8,128)(2,1)S(1)}) fusion(bf16[2,2,256,1024]{3,2,1,0:T(8,128)(2,1)} %collective-permute-done.5, bf16[2,2,4,64,1024]{4,3,2,1,0:T(8,128)(2,1)S(1)} %copy.8, pred[]{:T(512)S(6)} %eq.19, bf16[2,2,256,1024]{3,2,1,0:T(8,128)(2,1)} %collective-permute-done.6, ...), kind=kLoop, calls=%fused_computation.12 | loop fusion | flops 2097152 | bytes 10485762 | tf_op jit(solution)/shard_map/jit(_where)/select_n | solution.py:86
  123.1 4.6 %pad_maximum_fusion.refs_0_.refs_1_.refs_2_.refs_3_.refs_4_.refs_5_.refs_6_.refs_7_ = bf16[2,6,256,1024]{3,2,1,0:T(8,128)(2,1)} fusion(bf16[2,2,256,1024]{3,2,1,0:T(8,128)(2,1)S(1)} %get-tuple-element.10, bf16[2,2,256,1024]{3,2,1,0:T(8,128)(2,1)} %param.11, bf16[2,2,256,1024]{3,2,1,0:T(8,128)(2,1)S(1)} %get-tuple-element.9), kind=kLoop, calls=%fused_computation.1 | loop fusion | flops 6291456 | bytes 12582912 | tf_op jit(solution)/shard_map/concatenate | solution.py:119
  127.7 12.0 %shard_map.73 = bf16[256,1024]{1,0:T(8,128)(2,1)} custom-call(s32[4]{0:T(128)} %clamp_bitcast_fusion.slots_ref, s32[1]{0:T(128)S(6)} %copy.9.count_ref, bf16[256,1024]{1,0:T(8,128)(2,1)} %fusion.11.q_ref, bf16[2,6,256,1024]{3,2,1,0:T(8,128)(2,1)} %pad_maximum_fusion.refs_0_.refs_1_.refs_2_.refs_3_.refs_4_.refs_5_.refs_6_.refs_7_, ...), custom_call_target="tpu_custom_call" | custom-call | tf_op jit(solution)/shard_map/pallas_call | solution.py:49
  139.7 0.0 copy-start.1
  139.7 0.0 collective-permute-done.7
  139.7 1.4 broadcast_select_fusion.1
  141.1 0.0 copy-done.1
  141.1 1.5 %fusion.14 = bf16[256,1024]{1,0:T(8,128)(2,1)} fusion(bf16[256,1024]{1,0:T(8,128)(2,1)S(1)} %copy-done.1, bf16[1024,512]{1,0:T(8,128)(2,1)S(1)} %get-tuple-element.8, bf16[1024,512]{1,0:T(8,128)(2,1)S(1)} %get-tuple-element.7), kind=kOutput, calls=%fused_computation.18 | convolution fusion | flops 541327360 | bytes 3145728 | tf_op jit(solution)/shard_map/dot_general | solution.py:124
  (7 shorter events, 0.1 us)
Async XLA Ops:
  0.0 0.8 copy-start
  0.0 44.5 %copy-start.4 = (bf16[1024]{0:T(1024)(128)(2,1)S(1)}, bf16[1024]{0:T(1024)(128)(2,1)}, u32[]{:S(2)}) copy-start(bf16[1024]{0:T(1024)(128)(2,1)} %param.8) | copy-start | bytes 6148
  0.0 44.6 %copy-start.3 = (bf16[1024,32]{0,1:T(8,128)(2,1)S(1)}, bf16[1024,32]{0,1:T(8,128)(2,1)}, u32[]{:S(2)}) copy-start(bf16[1024,32]{0,1:T(8,128)(2,1)} %param.10) | copy-start | bytes 196612
  0.0 44.6 %copy-start.2 = (bf16[256,1024]{1,0:T(8,128)(2,1)S(1)}, bf16[256,1024]{1,0:T(8,128)(2,1)}, u32[]{:S(2)}) copy-start(bf16[256,1024]{1,0:T(8,128)(2,1)} %param.7) | copy-start | bytes 1572868
  41.2 5.6 %collective-permute-start = (bf16[1024,512]{1,0:T(8,128)(2,1)S(1)}, bf16[1024,512]{1,0:T(8,128)(2,1)S(1)}, u32[]{:S(2)}, u32[]{:S(2)}) collective-permute-start(bf16[1024,512]{1,0:T(8,128)(2,1)S(1)} %bitcast.23), channel_id=1, source_target_pairs={{0,32},{32,0},{64,96},{96,64},{128,160},{160,128},{192,224},{224,1... | collective-permute-start | bytes 3145736 | tf_op jit(solution)/shard_map/ppermute | solution.py:101
  48.6 17.4 %copy-start.5 = (s32[1,4]{1,0:T(1,128)S(1)}, s32[1,4]{1,0:T(1,128)}, u32[]{:S(2)}) copy-start(s32[1,4]{1,0:T(1,128)} %param.12) | copy-start | bytes 52
  49.7 33.0 %all-to-all-start.1 = ((bf16[32,32,512]{2,1,0:T(8,128)(2,1)}), bf16[32,32,512]{2,1,0:T(8,128)(2,1)S(1)}, u32[]{:S(2)}, u32[]{:S(2)}) async-start(bf16[32,32,512]{2,1,0:T(8,128)(2,1)} %tile.5), calls=%async_computation.1 | async-start | bytes 2097152 | tf_op jit(solution)/shard_map/all_to_all | solution.py:98
  55.5 65.0 %collective-permute-start.5 = (bf16[2,2,256,1024]{3,2,1,0:T(8,128)(2,1)}, bf16[2,2,256,1024]{3,2,1,0:T(8,128)(2,1)}, u32[]{:S(2)}, u32[]{:S(2)}) collective-permute-start(bf16[2,2,256,1024]{3,2,1,0:T(8,128)(2,1)} %param.11), channel_id=1, source_target_pairs={{0,32},{1,33},{2,34},{3,35},{4,36},{5,37},{6,38},{7,39},{8,40},{9,... | collective-permute-start | bytes 6291464 | tf_op jit(solution)/shard_map/ppermute | solution.py:66
  59.4 61.0 %collective-permute-start.6 = (bf16[2,2,256,1024]{3,2,1,0:T(8,128)(2,1)}, bf16[2,2,256,1024]{3,2,1,0:T(8,128)(2,1)}, u32[]{:S(2)}, u32[]{:S(2)}) collective-permute-start(bf16[2,2,256,1024]{3,2,1,0:T(8,128)(2,1)} %param.11), channel_id=1, source_target_pairs={{32,0},{33,1},{34,2},{35,3},{36,4},{37,5},{38,6},{39,7},{40,8},{41... | collective-permute-start | bytes 6291464 | tf_op jit(solution)/shard_map/ppermute | solution.py:67
  62.5 1.4 collective-permute-start.1
  63.8 2.7 %collective-permute-start.2 = (bf16[2,2,64,1024]{3,2,1,0:T(8,128)(2,1)S(1)}, bf16[2,2,64,1024]{3,2,1,0:T(8,128)(2,1)S(1)}, u32[]{:S(2)}, u32[]{:S(2)}) collective-permute-start(bf16[2,2,64,1024]{3,2,1,0:T(8,128)(2,1)S(1)} %collective-permute-done.1), channel_id=1, source_target_pairs={{224,225},{225,226},{226,227},{227,224},{228,229},{229,230},{230,2... | collective-permute-start | bytes 1572872 | tf_op jit(solution)/shard_map/ppermute | solution.py:82
  64.6 2.0 %collective-permute-start.3 = (bf16[2,2,64,1024]{3,2,1,0:T(8,128)(2,1)S(1)}, bf16[2,2,64,1024]{3,2,1,0:T(8,128)(2,1)S(1)}, u32[]{:S(2)}, u32[]{:S(2)}) collective-permute-start(bf16[2,2,64,1024]{3,2,1,0:T(8,128)(2,1)S(1)} %collective-permute-done.1), channel_id=1, source_target_pairs={{224,226},{225,227},{226,224},{227,225},{228,230},{229,231},{230,2... | collective-permute-start | bytes 1572872 | tf_op jit(solution)/shard_map/ppermute | solution.py:82
  65.3 1.3 collective-permute-start.4
  82.7 57.0 %collective-permute-start.7 = (bf16[1024,512]{1,0:T(8,128)(2,1)S(1)}, bf16[1024,512]{1,0:T(8,128)(2,1)}, u32[]{:S(2)}, u32[]{:S(2)}) collective-permute-start(bf16[1024,512]{1,0:T(8,128)(2,1)S(1)} %bitcast.22), channel_id=1, source_target_pairs={{0,32},{32,0},{64,96},{96,64},{128,160},{160,128},{192,224},{224,1... | collective-permute-start | bytes 3145736 | tf_op jit(solution)/shard_map/ppermute | solution.py:101
  139.7 1.4 %copy-start.1 = (bf16[256,1024]{1,0:T(8,128)(2,1)S(1)}, bf16[256,1024]{1,0:T(8,128)(2,1)}, u32[]{:S(2)}) copy-start(bf16[256,1024]{1,0:T(8,128)(2,1)} %shard_map.73) | copy-start | bytes 1572868
